TPU v7x, 512 devices: a whole 4x4x16 slice. The times are simulated.
512 devices in a mesh: exp: 16 (over z), sky: 32 (over y, x, core).
Axes of the slice: x: 4, y: 4, z: 16, core: 2. Of those that a mesh axis runs over, the one named last changes fastest.
Arguments:
- sky_start: float32 [16, 128, 4096], P(None, None, 'sky'), may hold values from -6 to 6
- exposures: bfloat16 [16, 1024, 2, 128, 128], P('exp', 'sky'), may hold values from -16 to 16
- weights: bfloat16 [16, 1024, 2], P('exp', 'sky'), may hold values from 0.5 to 2
- footprint_owner: int32 [16, 1024, 1], P('exp', 'sky'), may hold values from 0 to 31; in each aligned block of 32 rows (0 to 31, 32 to 63, ..., all dimensions but the last counted through in order) at most 2 rows name the same one
- footprint_row: int32 [16, 1024], P('exp', 'sky'), may hold values from 0 to 15
- kernel_index: int32 [16, 1024, 2, 2], P('exp', 'sky'), may hold values from 0 to 7
- kernels: bfloat16 [8, 128, 128], replicated, may hold values from -1 to 1
Outputs:
- sky_image: float32 [16, 128, 4096], P(None, None, 'sky')
Inputs may be any that keep to these rules, and one draw needn't show every extreme that they name: `footprint_owner`: the 32 footprint tiles of one device name one tile column at most 2 times, and some tile column exactly 2 times.
All inputs are finite; a program needn't handle non-finite values.
Results may differ from a plain program's by a relative error of at most 0.0035.
Values may be sent and summed in bfloat16 or wider, within the bound.
No kernel may reach another device: no remote copies, remote signals or barrier semaphores. Data moves between devices by JAX's collectives and lax.ppermute only.
A program may use at most 128 MiB of HBM per device.

v0:
```python
import jax
import jax.numpy as jnp
from jax import lax
from jax.sharding import PartitionSpec as P

ITERS = 2
weight_ceiling = 2.0


def padded_2(cells, sides, width):
    for axis, dim in sides:
        count = lax.axis_size(axis)
        ends = count - 1
        head = lax.slice_in_dim(cells, 0, width, axis=dim)
        tail = lax.slice_in_dim(cells, cells.shape[dim] - width, cells.shape[dim], axis=dim)
        cells = jnp.concatenate(
            [
                lax.ppermute(tail, axis, [(i, (i + 1) % count) for i in range(ends)]),
                cells,
                lax.ppermute(head, axis, [((i + 1) % count, i) for i in range(ends)]),
            ],
            axis=dim,
        )
    return cells


def pick_kernels(kernel_ids, kernels):
    table_size = kernels.shape[0]
    tile_edge = kernels.shape[1]
    onehot = (kernel_ids[..., None] == jnp.arange(table_size, dtype=jnp.int32)).astype(jnp.bfloat16)
    onehot = onehot.reshape(-1, table_size)
    selected = jnp.dot(onehot, kernels.reshape(table_size, -1), preferred_element_type=jnp.float32)
    selected = selected.astype(jnp.bfloat16).reshape(kernel_ids.shape + (tile_edge, tile_edge))
    return (selected[..., 0, :, :], selected[..., 1, :, :])


def adjoint_tiles(fetched, left_kernels, right_kernels, tile_weights, observed):
    left_product = jnp.einsum(
        "fetu,fuv->fetv", left_kernels, fetched, preferred_element_type=jnp.float32
    ).astype(jnp.bfloat16)
    predicted = jnp.einsum(
        "fetv,fewv->fetw", left_product, right_kernels, preferred_element_type=jnp.float32
    )
    residual = tile_weights.astype(jnp.float32)[..., None, None] * (
        predicted - observed.astype(jnp.float32)
    )
    residual = residual.astype(jnp.bfloat16)
    back_product = jnp.einsum(
        "feut,feuw->fetw", left_kernels, residual, preferred_element_type=jnp.float32
    ).astype(jnp.bfloat16)
    summed = jnp.sum(
        jnp.einsum(
            "fetw,fewv->fetv", back_product, right_kernels, preferred_element_type=jnp.float32
        ),
        axis=1,
    )
    return summed.astype(jnp.bfloat16)


def laplace_image(padded):
    image_rows = padded.reshape(padded.shape[0] * padded.shape[1], padded.shape[2])
    center = image_rows[:, 1:-1]
    vertical = jnp.pad(center, ((1, 1), (0, 0)))
    laplacian = 4.0 * center - image_rows[:, :-2] - image_rows[:, 2:] - vertical[:-2] - vertical[2:]
    return laplacian.reshape(padded.shape[0], padded.shape[1], padded.shape[2] - 2)


def per_device(
    sky_start, exposures, weights, footprint_owner, footprint_row, kernel_index, kernels
):
    sky_rows = sky_start.shape[0]
    tile_edge = sky_start.shape[1]
    foot_tiles = footprint_row.shape[1]
    expo_count = exposures.shape[2]
    n_sky = lax.axis_size("sky")
    n_exp = lax.axis_size("exp")
    capacity = max(2, 3 * foot_tiles // (2 * n_sky))
    slot_count = n_sky * capacity
    prior_weight = n_exp * foot_tiles * expo_count / (8.0 * sky_rows)
    owner_ids = footprint_owner[0, :, 0]
    tile_rows = footprint_row[0]
    onehot_owner = (owner_ids[:, None] == jnp.arange(n_sky, dtype=jnp.int32)[None, :]).astype(
        jnp.int32
    )
    ranks = jnp.sum((jnp.cumsum(onehot_owner, axis=0) - onehot_owner) * onehot_owner, axis=1)
    slot_of = owner_ids * capacity + ranks
    packing = jnp.arange(slot_count, dtype=jnp.int32)[:, None] == slot_of[None, :]
    requested = jnp.sum(jnp.where(packing, tile_rows[None, :] + 1, 0), axis=1) - 1
    slot_source = jnp.sum(jnp.where(packing, jnp.arange(foot_tiles)[None, :] + 1, 0), axis=1) - 1
    slot_source = jnp.where(slot_source < 0, foot_tiles, slot_source)
    observed = exposures[0]
    tile_weights = weights[0]
    kernel_ids = kernel_index[0]
    incoming = lax.all_to_all(requested, "sky", split_axis=0, concat_axis=0, tiled=True)
    left_kernels, right_kernels = pick_kernels(kernel_ids, kernels)
    receive_map = jnp.arange(sky_rows, dtype=jnp.int32)[:, None] == incoming[None, :]
    local_counts = float(expo_count) * jnp.sum(receive_map.astype(jnp.float32), axis=1)
    receive_half = receive_map.astype(jnp.bfloat16)
    safe_rows = jnp.maximum(incoming, 0)
    rows_per = sky_rows // n_exp
    own_rows = lax.axis_index("exp") * rows_per
    count_tile = jnp.broadcast_to(local_counts[:, None], (sky_rows, tile_edge))
    sky_now = sky_start
    for iteration in range(ITERS):
        replies = lax.all_to_all(
            sky_now[safe_rows].astype(jnp.bfloat16), "sky", split_axis=0, concat_axis=0, tiled=True
        )
        fetched = replies[slot_of]
        adjoint = adjoint_tiles(fetched, left_kernels, right_kernels, tile_weights, observed)
        outgoing = jnp.where(
            (slot_source < foot_tiles)[:, None, None],
            adjoint[jnp.minimum(slot_source, foot_tiles - 1)],
            jnp.zeros((), adjoint.dtype),
        )
        arrived = lax.all_to_all(outgoing, "sky", split_axis=0, concat_axis=0, tiled=True)
        if iteration == 0:
            count_tiles = lax.all_gather(count_tile, "exp", axis=0, tiled=True)
            count_tiles, arrived = lax.optimization_barrier((count_tiles, arrived))
            counts = jnp.sum(
                count_tiles.astype(jnp.float32).reshape(n_exp, sky_rows, tile_edge)[:, :, 0], axis=0
            )
            denominator = weight_ceiling * counts + 8.0 * prior_weight
            own_denominator = lax.dynamic_slice_in_dim(denominator, own_rows, rows_per)
        partial_value = jnp.einsum(
            "rj,juv->ruv", receive_half, arrived, preferred_element_type=jnp.float32
        )
        payload = partial_value.astype(jnp.bfloat16).reshape(n_exp, rows_per * tile_edge, tile_edge)
        row_parts = lax.all_to_all(payload, "exp", split_axis=0, concat_axis=0, tiled=True)
        summed = jnp.sum(
            row_parts.astype(jnp.float32).reshape((n_exp,) + payload.shape[1:]), axis=0
        )
        own_total = summed[: rows_per * tile_edge].reshape(rows_per, tile_edge, tile_edge)
        scaled = own_total / own_denominator[:, None, None]
        gathered = lax.all_gather(scaled.astype(jnp.bfloat16), "exp", axis=0, tiled=True)
        laplacian = laplace_image(padded_2(sky_now, (("sky", 2),), 1))
        smooth = prior_weight * laplacian / denominator[:, None, None]
        sky_now = sky_now - (gathered.astype(jnp.float32) + smooth)
    return sky_now


def solution(mesh):
    in_specs = (
        P(None, None, "sky"),
        P("exp", "sky", None, None, None),
        P("exp", "sky", None),
        P("exp", "sky", None),
        P("exp", "sky"),
        P("exp", "sky", None, None),
        P(),
    )
    out_specs = P(None, None, "sky")
    return jax.shard_map(
        per_device, mesh=mesh, in_specs=in_specs, out_specs=out_specs, check_vma=False
    )
```

profile of v0, /device:TPU:2, one launch (start us, length us, event | category | flops | bytes accessed | tf_op | source)
XLA Modules:
  0.0 339.1 jit_solution(3702893933402710310)
XLA Ops:
  0.0 0.7 fusion.48
  0.8 0.8 select_reduce_fusion.2
  1.6 0.7 iota_add_fusion
  2.3 0.7 add_bitcast_fusion
  3.1 14.8 %all_to_all.36 = s32[32,2,1]{1,2,0:T(1,128)S(1)} all-to-all(s32[32,2,1]{1,2,0:T(1,128)S(1)} %bitcast.102), channel_id=1, replica_groups=mesh['exp'=16,'sky'=32] {'sky'}, dimensions={0} | all-to-all | bytes 512 | tf_op jit(solution)/shard_map/all_to_all | solution.py:94
  17.9 0.5 broadcast.253
  18.4 0.7 maximum_reduce_fusion
  19.3 3.3 gather_fusion
  22.6 5.2 %all-to-all-start.1 = ((bf16[64,128,128]{2,1,0:T(8,128)(2,1)}), bf16[64,128,128]{2,1,0:T(8,128)(2,1)S(1)}, u32[]{:S(2)}, u32[]{:S(2)}) async-start(bf16[64,128,128]{2,1,0:T(8,128)(2,1)} %gather_fusion), calls=%async_computation.1 | async-start | bytes 4194304 | tf_op jit(solution)/shard_map/all_to_all | solution.py:105
  28.2 1.3 fusion.4
  29.6 3.2 copy.109
  32.8 23.1 %all-to-all-done.1 = bf16[64,128,128]{2,1,0:T(8,128)(2,1)S(1)} async-done(((bf16[64,128,128]{2,1,0:T(8,128)(2,1)}), bf16[64,128,128]{2,1,0:T(8,128)(2,1)S(1)}, u32[]{:S(2)}, u32[]{:S(2)}) %all-to-all-start.1) | async-done | bytes 2097184 | tf_op jit(solution)/shard_map/all_to_all | solution.py:105
  55.8 0.7 gather_fusion.1
  56.6 5.0 %fusion.1 = bf16[32,2,128,128]{3,2,1,0:T(8,128)(2,1)S(1)} fusion(bf16[1,32,2,128,128]{4,3,2,1,0:T(8,128)(2,1)} %param.8, f32[32,2]{1,0:T(8,128)S(1)} %copy.80, bf16[32,2,2,128,128]{4,3,2,1,0:T(8,128)(2,1)} %bitcast.92, bf16[32,128,128]{2,1,0:T(8,128)(2,1)S(1)} %gather_fusion.1), kind=kOutput, calls=%fused_computation.10 | convolution fusion | flops 542113792 | bytes 9437440 | tf_op jit(solution)/shard_map/fetv,fewv->fetw/dot_general | solution.py:41
  61.6 3.6 %bitcast_convert_fusion.1 = bf16[32,128,128]{2,1,0:T(8,128)(2,1)S(1)} fusion(bf16[32,2,128,128]{3,2,1,0:T(8,128)(2,1)S(1)} %fusion.1, bf16[32,2,2,128,128]{4,3,2,1,0:T(8,128)(2,1)} %bitcast.93), kind=kOutput, calls=%fused_computation.19 | convolution fusion | flops 538443776 | bytes 7340032 | tf_op jit(solution)/shard_map/fetw,fewv->fetv/dot_general | solution.py:52
  65.3 1.0 gather_fusion.2
  66.2 1.5 broadcast_select_fusion.1
  67.8 6.0 %all-to-all-start.2 = ((bf16[64,128,128]{2,1,0:T(8,128)(2,1)}), bf16[64,128,128]{2,1,0:T(8,128)(2,1)S(1)}, u32[]{:S(2)}, u32[]{:S(2)}) async-start(bf16[64,128,128]{2,1,0:T(8,128)(2,1)} %broadcast_select_fusion.1), calls=%async_computation.2 | async-start | bytes 4194304 | tf_op jit(solution)/shard_map/all_to_all | solution.py:115
  73.8 1.3 dynamic-slice
  76.1 35.3 %all-reduce.2 = f32[256]{0:T(256)S(1)} all-reduce(f32[256]{0:T(256)S(1)} %multiply_dynamic-update-slice_fusion), channel_id=2, replica_groups=mesh['exp'=16,'sky'=32] {'exp'}, use_global_device_ids=true, to_apply=%add.2 | all-reduce | flops 256 | bytes 2048
  111.4 1.3 fusion.27
  112.7 0.9 copy.84
  113.6 6.8 %all-to-all-start.3 = ((bf16[16,128,128]{2,1,0:T(8,128)(2,1)}), bf16[16,128,128]{2,1,0:T(8,128)(2,1)}, u32[]{:S(2)}, u32[]{:S(2)}) async-start(bf16[16,128,128]{2,1,0:T(8,128)(2,1)} %copy.84), calls=%async_computation.3 | async-start | bytes 1048576 | tf_op jit(solution)/shard_map/all_to_all | solution.py:128
  120.4 0.4 fusion.59
  120.8 0.3 copy.107
  121.1 1.9 collective-permute-start.1
  123.4 2.6 collective-permute-start
  126.0 0.4 copy.89
  126.3 2.0 collective-permute-done
  128.3 0.4 copy.88
  128.7 0.9 pad_maximum_fusion
  129.6 0.3 slice.83
  129.9 0.5 fusion.38
  130.6 0.6 dynamic_slice.3
  131.1 15.0 %all-to-all-done.3 = bf16[16,128,128]{2,1,0:T(8,128)(2,1)} async-done(((bf16[16,128,128]{2,1,0:T(8,128)(2,1)}), bf16[16,128,128]{2,1,0:T(8,128)(2,1)}, u32[]{:S(2)}, u32[]{:S(2)}) %all-to-all-start.3) | async-done | bytes 524320 | tf_op jit(solution)/shard_map/all_to_all | solution.py:128
  146.1 1.1 convert_reduce_fusion.1
  147.3 0.6 divide_convert_fusion.1
  147.8 32.3 %all-gather = bf16[2048,128]{1,0:T(8,128)(2,1)S(1)} all-gather(bf16[128,128]{1,0:T(8,128)(2,1)S(1)} %divide_convert_fusion.1), channel_id=3, replica_groups=mesh['exp'=16,'sky'=32] {'exp'}, dimensions={0}, use_global_device_ids=true | all-gather | bytes 557056 | tf_op jit(solution)/shard_map/all_gather | solution.py:134
  180.4 2.1 gather_fusion.3
  182.5 33.0 %all_to_all.37 = bf16[64,128,128]{2,1,0:T(8,128)(2,1)} all-to-all(bf16[64,128,128]{2,1,0:T(8,128)(2,1)} %gather_fusion.3), channel_id=1, replica_groups=mesh['exp'=16,'sky'=32] {'sky'}, dimensions={0} | all-to-all | bytes 4194304 | tf_op jit(solution)/shard_map/all_to_all | solution.py:105
  215.5 2.3 gather_fusion.4
  217.8 6.3 %fusion.3 = bf16[32,2,128,128]{3,2,1,0:T(8,128)(2,1)} fusion(bf16[1,32,2,128,128]{4,3,2,1,0:T(8,128)(2,1)} %param.8, f32[32,2]{1,0:T(8,128)S(1)} %copy.80, bf16[32,2,2,128,128]{4,3,2,1,0:T(8,128)(2,1)} %bitcast.94, bf16[32,128,128]{2,1,0:T(8,128)(2,1)S(1)} %gather_fusion.4), kind=kOutput, calls=%fused_computation.12 | convolution fusion | flops 542113792 | bytes 9437440 | tf_op jit(solution)/shard_map/fetv,fewv->fetw/dot_general | solution.py:41
  224.2 4.3 %bitcast_convert_fusion = bf16[32,128,128]{2,1,0:T(8,128)(2,1)S(1)} fusion(bf16[32,2,128,128]{3,2,1,0:T(8,128)(2,1)} %fusion.3, bf16[32,2,2,128,128]{4,3,2,1,0:T(8,128)(2,1)} %bitcast.95), kind=kOutput, calls=%fused_computation.18 | convolution fusion | flops 538443776 | bytes 7340032 | tf_op jit(solution)/shard_map/fetw,fewv->fetv/dot_general | solution.py:52
  228.4 2.2 gather_fusion.5
  230.6 1.8 broadcast_select_fusion
  232.4 31.9 %all_to_all.38 = bf16[64,128,128]{2,1,0:T(8,128)(2,1)S(1)} all-to-all(bf16[64,128,128]{2,1,0:T(8,128)(2,1)S(1)} %broadcast_select_fusion), channel_id=1, replica_groups=mesh['exp'=16,'sky'=32] {'sky'}, dimensions={0} | all-to-all | bytes 4194304 | tf_op jit(solution)/shard_map/all_to_all | solution.py:115
  264.4 1.3 fusion.30
  265.6 0.9 copy.92
  266.5 6.7 %all-to-all-start.6 = ((bf16[16,128,128]{2,1,0:T(8,128)(2,1)}), bf16[16,128,128]{2,1,0:T(8,128)(2,1)}, u32[]{:S(2)}, u32[]{:S(2)}) async-start(bf16[16,128,128]{2,1,0:T(8,128)(2,1)} %copy.92), calls=%async_computation.6 | async-start | bytes 1048576 | tf_op jit(solution)/shard_map/all_to_all | solution.py:128
  273.2 0.4 fusion.58
  273.6 0.3 copy.94
  273.9 2.8 collective-permute-start.3
  277.1 2.1 collective-permute-start.2
  279.2 0.4 copy.96
  279.6 2.4 collective-permute-done.2
  282.0 0.4 copy.95
  282.4 0.9 pad_maximum_fusion.1
  283.3 0.3 slice.88
  283.6 0.5 fusion.35
  284.1 18.4 %all-to-all-done.6 = bf16[16,128,128]{2,1,0:T(8,128)(2,1)} async-done(((bf16[16,128,128]{2,1,0:T(8,128)(2,1)}), bf16[16,128,128]{2,1,0:T(8,128)(2,1)}, u32[]{:S(2)}, u32[]{:S(2)}) %all-to-all-start.6) | async-done | bytes 524320 | tf_op jit(solution)/shard_map/all_to_all | solution.py:128
  302.5 1.1 convert_reduce_fusion
  303.7 0.6 divide_convert_fusion
  304.2 33.6 %all-gather.1 = bf16[2048,128]{1,0:T(8,128)(2,1)S(1)} all-gather(bf16[128,128]{1,0:T(8,128)(2,1)S(1)} %divide_convert_fusion), channel_id=4, replica_groups=mesh['exp'=16,'sky'=32] {'exp'}, dimensions={0}, use_global_device_ids=true | all-gather | bytes 557056 | tf_op jit(solution)/shard_map/all_gather | solution.py:134
  337.9 1.2 fusion.39
  (38 shorter events, 2.2 us)
Async XLA Ops:
  22.6 5.3 %copy-start.4 = (bf16[1,32,2]{1,2,0:T(2,128)(2,1)S(1)}, bf16[1,32,2]{1,2,0:T(2,128)(2,1)}, u32[]{:S(2)}) copy-start(bf16[1,32,2]{1,2,0:T(2,128)(2,1)} %param.9) | copy-start | bytes 388
  22.6 5.4 %copy-start.3 = (s32[1,32,2,2]{1,3,2,0:T(2,128)S(1)}, s32[1,32,2,2]{1,3,2,0:T(2,128)}, u32[]{:S(2)}) copy-start(s32[1,32,2,2]{1,3,2,0:T(2,128)} %param.12) | copy-start | bytes 1540
  22.6 5.6 %copy-start.1 = (bf16[8,128,128]{2,1,0:T(8,128)(2,1)S(1)}, bf16[8,128,128]{2,1,0:T(8,128)(2,1)}, u32[]{:S(2)}) copy-start(bf16[8,128,128]{2,1,0:T(8,128)(2,1)} %param.13) | copy-start | bytes 786436
  22.6 33.2 %all-to-all-start.1 = ((bf16[64,128,128]{2,1,0:T(8,128)(2,1)}), bf16[64,128,128]{2,1,0:T(8,128)(2,1)S(1)}, u32[]{:S(2)}, u32[]{:S(2)}) async-start(bf16[64,128,128]{2,1,0:T(8,128)(2,1)} %gather_fusion), calls=%async_computation.1 | async-start | bytes 4194304 | tf_op jit(solution)/shard_map/all_to_all | solution.py:105
  29.5 3.2 copy-start.2
  67.8 43.6 %all-to-all-start.2 = ((bf16[64,128,128]{2,1,0:T(8,128)(2,1)}), bf16[64,128,128]{2,1,0:T(8,128)(2,1)S(1)}, u32[]{:S(2)}, u32[]{:S(2)}) async-start(bf16[64,128,128]{2,1,0:T(8,128)(2,1)} %broadcast_select_fusion.1), calls=%async_computation.2 | async-start | bytes 4194304 | tf_op jit(solution)/shard_map/all_to_all | solution.py:115
  111.4 9.0 %copy-start = (f32[16,128,128]{2,1,0:T(8,128)S(1)}, f32[16,128,128]{2,1,0:T(8,128)}, u32[]{:S(2)}) copy-start(f32[16,128,128]{2,1,0:T(8,128)} %param.7) | copy-start | bytes 3145732
  113.6 32.5 %all-to-all-start.3 = ((bf16[16,128,128]{2,1,0:T(8,128)(2,1)}), bf16[16,128,128]{2,1,0:T(8,128)(2,1)}, u32[]{:S(2)}, u32[]{:S(2)}) async-start(bf16[16,128,128]{2,1,0:T(8,128)(2,1)} %copy.84), calls=%async_computation.3 | async-start | bytes 1048576 | tf_op jit(solution)/shard_map/all_to_all | solution.py:128
  121.1 4.9 %collective-permute-start.1 = (f32[16,128,1]{1,0,2:T(8,128)S(1)}, f32[16,128,1]{1,0,2:T(8,128)S(1)}, u32[]{:S(2)}, u32[]{:S(2)}) collective-permute-start(f32[16,128,1]{1,0,2:T(8,128)S(1)} %copy.107), channel_id=1, source_target_pairs={{1,0},{2,1},{3,2},{4,3},{5,4},{6,5},{7,6},{8,7},{9,8},{10,9},{11,1... | collective-permute-start | bytes 24584 | tf_op jit(solution)/shard_map/ppermute | solution.py:20
  123.4 5.0 %collective-permute-start = (f32[16,128,1]{1,0,2:T(8,128)S(1)}, f32[16,128,1]{1,0,2:T(8,128)S(1)}, u32[]{:S(2)}, u32[]{:S(2)}) collective-permute-start(f32[16,128,1]{1,0,2:T(8,128)S(1)} %copy.106), channel_id=1, source_target_pairs={{0,1},{1,2},{2,3},{3,4},{4,5},{5,6},{6,7},{7,8},{8,9},{9,10},{10,1... | collective-permute-start | bytes 24584 | tf_op jit(solution)/shard_map/ppermute | solution.py:18
  266.5 36.0 %all-to-all-start.6 = ((bf16[16,128,128]{2,1,0:T(8,128)(2,1)}), bf16[16,128,128]{2,1,0:T(8,128)(2,1)}, u32[]{:S(2)}, u32[]{:S(2)}) async-start(bf16[16,128,128]{2,1,0:T(8,128)(2,1)} %copy.92), calls=%async_computation.6 | async-start | bytes 1048576 | tf_op jit(solution)/shard_map/all_to_all | solution.py:128
  273.9 5.3 %collective-permute-start.3 = (f32[16,128,1]{1,0,2:T(8,128)S(1)}, f32[16,128,1]{1,0,2:T(8,128)S(1)}, u32[]{:S(2)}, u32[]{:S(2)}) collective-permute-start(f32[16,128,1]{1,0,2:T(8,128)S(1)} %copy.94), channel_id=1, source_target_pairs={{1,0},{2,1},{3,2},{4,3},{5,4},{6,5},{7,6},{8,7},{9,8},{10,9},{11,1... | collective-permute-start | bytes 24584 | tf_op jit(solution)/shard_map/ppermute | solution.py:20
  277.1 5.0 %collective-permute-start.2 = (f32[16,128,1]{1,0,2:T(8,128)S(1)}, f32[16,128,1]{1,0,2:T(8,128)S(1)}, u32[]{:S(2)}, u32[]{:S(2)}) collective-permute-start(f32[16,128,1]{1,0,2:T(8,128)S(1)} %copy.93), channel_id=1, source_target_pairs={{0,1},{1,2},{2,3},{3,4},{4,5},{5,6},{6,7},{7,8},{8,9},{9,10},{10,1... | collective-permute-start | bytes 24584 | tf_op jit(solution)/shard_map/ppermute | solution.py:18
where the time goes:
time: 340 us; the launch traced here: 339 us
  blocking collectives  181 us (53%)
  waiting for transfers between devices  60.9 us (18%)
  starting transfers between devices  34.2 us (10%)
  local copies, waits for them, and re-layouts  23.9 us (7%)
  matrix products  23.1 us (7%)
  other arithmetic  15.1 us (4%)
    all_gather x2, blocking collectives, per_device(): lax.all_gather(scaled.astype(jnp.bfloat16), 'exp', axis=0, tiled=True)  65.9 us
    unnamed x1, blocking collectives  35.3 us
    all_to_all x2, waiting for transfers between devices, per_device(): lax.all_to_all(payload, 'exp', split_axis=0, concat_axis=0, tiled=True)  33.4 us
    all_to_all x1, blocking collectives, per_device(): lax.all_to_all(sky_now[safe_rows].astype(jnp.bfloat16), 'sky', split_axis...  33 us
    all_to_all x1, blocking collectives, per_device(): lax.all_to_all(outgoing, 'sky', split_axis=0, concat_axis=0, tiled=True)  31.9 us
    all_to_all x1, waiting for transfers between devices, per_device(): lax.all_to_all(sky_now[safe_rows].astype(jnp.bfloat16), 'sky', split_axis...  23.1 us
    all_to_all x1, blocking collectives, per_device(): lax.all_to_all(requested, 'sky', split_axis=0, concat_axis=0, tiled=True)  14.8 us
    all_to_all x2, starting transfers between devices, per_device(): lax.all_to_all(payload, 'exp', split_axis=0, concat_axis=0, tiled=True)  13.5 us
  transfers between devices with their start and end apart: 8, of which 5 were waited for; matrix products, arithmetic and copies ran while one was open for 4% of the time, Pallas kernels for 0%

commit v1 on v0

--- a/solution.py
+++ b/solution.py
@@ -5,6 +5,12 @@
 
 ITERS = 2
 weight_ceiling = 2.0
+
+
+def in_order(pieces, dim):
+    lengths = list(pieces.shape[1:])
+    lengths[dim] *= pieces.shape[0]
+    return jnp.moveaxis(pieces, 0, dim).reshape(lengths)
 
 
 def padded_2(cells, sides, width):
@@ -131,7 +137,20 @@
         )
         own_total = summed[: rows_per * tile_edge].reshape(rows_per, tile_edge, tile_edge)
         scaled = own_total / own_denominator[:, None, None]
-        gathered = lax.all_gather(scaled.astype(jnp.bfloat16), "exp", axis=0, tiled=True)
+        x = scaled.astype(jnp.bfloat16)
+        peers = lax.axis_size("exp")
+        pairs = [(i_2, (i_2 + 1) % peers) for i_2 in range(peers)]
+        back = [(b, a) for a, b in pairs]
+        lower, upper = ([], [])
+        for step in range(peers - 1):
+            if step % 2 == 0:
+                lower.append(lax.ppermute(lower[-1] if lower else x, "exp", pairs))
+            else:
+                upper.append(lax.ppermute(upper[-1] if upper else x, "exp", back))
+        blocks = jnp.stack([*lower[::-1], x, *upper])
+        shift = lax.axis_index("exp") - len(lower)
+        blocks = blocks[(jnp.arange(peers) - shift) % peers]
+        gathered = in_order(blocks, 0)
         laplacian = laplace_image(padded_2(sky_now, (("sky", 2),), 1))
         smooth = prior_weight * laplacian / denominator[:, None, None]
         sky_now = sky_now - (gathered.astype(jnp.float32) + smooth)

time: 340 us -> 418 us (1.23)
  the two profiles are of different devices: /device:TPU:2 before, /device:TPU:8 now
where the time goes in v1:
time: 418 us; the launch traced here: 416 us
  blocking collectives  152 us (36%)
  starting transfers between devices  133 us (32%)
  waiting for transfers between devices  61.9 us (15%)
  local copies, waits for them, and re-layouts  27.5 us (7%)
  matrix products  23.1 us (6%)
  other arithmetic  16.1 us (4%)
    ppermute x14, starting transfers between devices, per_device(): upper.append(lax.ppermute(upper[-1] if upper else x, 'exp', back))  71.8 us
    all_to_all x1, blocking collectives, per_device(): lax.all_to_all(payload, 'exp', split_axis=0, concat_axis=0, tiled=True)  37.7 us
    unnamed x1, blocking collectives  35.3 us
    ppermute x16, starting transfers between devices, per_device(): lower.append(lax.ppermute(lower[-1] if lower else x, 'exp', pairs))  33.4 us
    all_to_all x1, blocking collectives, per_device(): lax.all_to_all(sky_now[safe_rows].astype(jnp.bfloat16), 'sky', split_axis...  32.8 us
    all_to_all x1, blocking collectives, per_device(): lax.all_to_all(outgoing, 'sky', split_axis=0, concat_axis=0, tiled=True)  31.9 us
    all_to_all x1, waiting for transfers between devices, per_device(): lax.all_to_all(payload, 'exp', split_axis=0, concat_axis=0, tiled=True)  25 us
    all_to_all x1, waiting for transfers between devices, per_device(): lax.all_to_all(sky_now[safe_rows].astype(jnp.bfloat16), 'sky', split_axis...  21.6 us
  transfers between devices with their start and end apart: 37, of which 7 were waited for; matrix products, arithmetic and copies ran while one was open for 4% of the time, Pallas kernels for 0%

profile of v1, /device:TPU:8, one launch (start us, length us, event | category | flops | bytes accessed | tf_op | source)
XLA Modules:
  0.0 416.1 jit_solution(1886781331999272653)
XLA Ops:
  3.1 14.7 %all_to_all.36 = s32[32,2,1]{1,2,0:T(1,128)S(1)} all-to-all(s32[32,2,1]{1,2,0:T(1,128)S(1)} %bitcast.200), channel_id=1, replica_groups=mesh['exp'=16,'sky'=32] {'sky'}, dimensions={0} | all-to-all | bytes 512 | tf_op jit(solution)/shard_map/all_to_all | solution.py:100
  19.3 3.3 gather_fusion
  22.6 5.3 %all-to-all-start.1 = ((bf16[64,128,128]{2,1,0:T(8,128)(2,1)}), bf16[64,128,128]{2,1,0:T(8,128)(2,1)S(1)}, u32[]{:S(2)}, u32[]{:S(2)}) async-start(bf16[64,128,128]{2,1,0:T(8,128)(2,1)} %gather_fusion), calls=%async_computation.1 | async-start | bytes 4194304 | tf_op jit(solution)/shard_map/all_to_all | solution.py:111
  28.3 1.3 fusion.4
  29.6 3.2 copy.148
  32.8 21.6 %all-to-all-done.1 = bf16[64,128,128]{2,1,0:T(8,128)(2,1)S(1)} async-done(((bf16[64,128,128]{2,1,0:T(8,128)(2,1)}), bf16[64,128,128]{2,1,0:T(8,128)(2,1)S(1)}, u32[]{:S(2)}, u32[]{:S(2)}) %all-to-all-start.1) | async-done | bytes 2097184 | tf_op jit(solution)/shard_map/all_to_all | solution.py:111
  55.1 5.0 %fusion.1 = bf16[32,2,128,128]{3,2,1,0:T(8,128)(2,1)S(1)} fusion(bf16[1,32,2,128,128]{4,3,2,1,0:T(8,128)(2,1)} %param.8, f32[32,2]{1,0:T(8,128)S(1)} %copy.104, bf16[32,2,2,128,128]{4,3,2,1,0:T(8,128)(2,1)} %bitcast.190, bf16[32,128,128]{2,1,0:T(8,128)(2,1)S(1)} %gather_fusion.1), kind=kOutput, calls=%fused_computation.12 | convolution fusion | flops 542113792 | bytes 9437440 | tf_op jit(solution)/shard_map/fetv,fewv->fetw/dot_general | solution.py:47
  60.2 3.6 bitcast_convert_fusion.1
  64.8 1.6 broadcast_select_fusion.1
  66.4 7.5 %all-to-all-start.2 = ((bf16[64,128,128]{2,1,0:T(8,128)(2,1)}), bf16[64,128,128]{2,1,0:T(8,128)(2,1)S(1)}, u32[]{:S(2)}, u32[]{:S(2)}) async-start(bf16[64,128,128]{2,1,0:T(8,128)(2,1)} %broadcast_select_fusion.1), calls=%async_computation.2 | async-start | bytes 4194304 | tf_op jit(solution)/shard_map/all_to_all | solution.py:121
  73.9 1.3 dynamic-slice
  76.1 35.3 %all-reduce.2 = f32[256]{0:T(256)S(1)} all-reduce(f32[256]{0:T(256)S(1)} %multiply_dynamic-update-slice_fusion), channel_id=2, replica_groups=mesh['exp'=16,'sky'=32] {'exp'}, use_global_device_ids=true, to_apply=%add.2 | all-reduce | flops 256 | bytes 2048
  111.5 1.3 fusion.27
  113.7 6.7 %all-to-all-start.3 = ((bf16[16,128,128]{2,1,0:T(8,128)(2,1)}), bf16[16,128,128]{2,1,0:T(8,128)(2,1)S(1)}, u32[]{:S(2)}, u32[]{:S(2)}) async-start(bf16[16,128,128]{2,1,0:T(8,128)(2,1)} %copy.108), calls=%async_computation.3 | async-start | bytes 1048576 | tf_op jit(solution)/shard_map/all_to_all | solution.py:134
  121.2 25.0 %all-to-all-done.3 = bf16[16,128,128]{2,1,0:T(8,128)(2,1)S(1)} async-done(((bf16[16,128,128]{2,1,0:T(8,128)(2,1)}), bf16[16,128,128]{2,1,0:T(8,128)(2,1)S(1)}, u32[]{:S(2)}, u32[]{:S(2)}) %all-to-all-start.3) | async-done | bytes 524320 | tf_op jit(solution)/shard_map/all_to_all | solution.py:134
  146.9 2.2 collective-permute-start
  149.2 4.8 %collective-permute-done = bf16[1,128,128]{2,1,0:T(8,128)(2,1)S(1)} collective-permute-done((bf16[1,128,128]{2,1,0:T(8,128)(2,1)S(1)}, bf16[1,128,128]{2,1,0:T(8,128)(2,1)S(1)}, u32[]{:S(2)}, u32[]{:S(2)}) %collective-permute-start) | collective-permute-done | bytes 32800 | tf_op jit(solution)/shard_map/ppermute | solution.py:147
  153.9 2.4 collective-permute-start.1
  156.3 4.7 %collective-permute-start.8 = (bf16[1,128,128]{2,1,0:T(8,128)(2,1)S(1)}, bf16[1,128,128]{2,1,0:T(8,128)(2,1)S(1)}, u32[]{:S(2)}, u32[]{:S(2)}) collective-permute-start(bf16[1,128,128]{2,1,0:T(8,128)(2,1)S(1)} %fusion.60), channel_id=1, source_target_pairs={{32,0},{64,32},{96,64},{128,96},{160,128},{192,160},{224,192},{256... | collective-permute-start | bytes 98312 | tf_op jit(solution)/shard_map/ppermute | solution.py:149
  161.0 1.9 collective-permute-start.2
  162.9 5.1 %collective-permute-start.9 = (bf16[1,128,128]{2,1,0:T(8,128)(2,1)S(1)}, bf16[1,128,128]{2,1,0:T(8,128)(2,1)S(1)}, u32[]{:S(2)}, u32[]{:S(2)}) collective-permute-start(bf16[1,128,128]{2,1,0:T(8,128)(2,1)S(1)} %collective-permute-done.8), channel_id=1, source_target_pairs={{32,0},{64,32},{96,64},{128,96},{160,128},{192,160},{224,192},{256... | collective-permute-start | bytes 98312 | tf_op jit(solution)/shard_map/ppermute | solution.py:149
  168.1 1.9 collective-permute-start.3
  171.3 1.9 collective-permute-start.16
  173.6 2.4 collective-permute-start.15
  176.0 5.1 %collective-permute-start.10 = (bf16[1,128,128]{2,1,0:T(8,128)(2,1)S(1)}, bf16[1,128,128]{2,1,0:T(8,128)(2,1)S(1)}, u32[]{:S(2)}, u32[]{:S(2)}) collective-permute-start(bf16[1,128,128]{2,1,0:T(8,128)(2,1)S(1)} %collective-permute-done.9), channel_id=1, source_target_pairs={{32,0},{64,32},{96,64},{128,96},{160,128},{192,160},{224,192},{256... | collective-permute-start | bytes 98312 | tf_op jit(solution)/shard_map/ppermute | solution.py:149
  181.2 1.9 collective-permute-start.4
  183.1 5.2 %collective-permute-start.11 = (bf16[1,128,128]{2,1,0:T(8,128)(2,1)S(1)}, bf16[1,128,128]{2,1,0:T(8,128)(2,1)S(1)}, u32[]{:S(2)}, u32[]{:S(2)}) collective-permute-start(bf16[1,128,128]{2,1,0:T(8,128)(2,1)S(1)} %collective-permute-done.10), channel_id=1, source_target_pairs={{32,0},{64,32},{96,64},{128,96},{160,128},{192,160},{224,192},{256... | collective-permute-start | bytes 98312 | tf_op jit(solution)/shard_map/ppermute | solution.py:149
  188.4 1.9 collective-permute-start.5
  192.4 5.1 %collective-permute-start.12 = (bf16[1,128,128]{2,1,0:T(8,128)(2,1)S(1)}, bf16[1,128,128]{2,1,0:T(8,128)(2,1)S(1)}, u32[]{:S(2)}, u32[]{:S(2)}) collective-permute-start(bf16[1,128,128]{2,1,0:T(8,128)(2,1)S(1)} %collective-permute-done.11), channel_id=1, source_target_pairs={{32,0},{64,32},{96,64},{128,96},{160,128},{192,160},{224,192},{256... | collective-permute-start | bytes 98312 | tf_op jit(solution)/shard_map/ppermute | solution.py:149
  197.5 2.1 collective-permute-start.6
  200.8 5.1 %collective-permute-start.13 = (bf16[1,128,128]{2,1,0:T(8,128)(2,1)S(1)}, bf16[1,128,128]{2,1,0:T(8,128)(2,1)S(1)}, u32[]{:S(2)}, u32[]{:S(2)}) collective-permute-start(bf16[1,128,128]{2,1,0:T(8,128)(2,1)S(1)} %collective-permute-done.12), channel_id=1, source_target_pairs={{32,0},{64,32},{96,64},{128,96},{160,128},{192,160},{224,192},{256... | collective-permute-start | bytes 98312 | tf_op jit(solution)/shard_map/ppermute | solution.py:149
  206.0 1.9 collective-permute-start.7
  208.4 5.1 %collective-permute-start.14 = (bf16[1,128,128]{2,1,0:T(8,128)(2,1)S(1)}, bf16[1,128,128]{2,1,0:T(8,128)(2,1)S(1)}, u32[]{:S(2)}, u32[]{:S(2)}) collective-permute-start(bf16[1,128,128]{2,1,0:T(8,128)(2,1)S(1)} %collective-permute-done.13), channel_id=1, source_target_pairs={{32,0},{64,32},{96,64},{128,96},{160,128},{192,160},{224,192},{256... | collective-permute-start | bytes 98312 | tf_op jit(solution)/shard_map/ppermute | solution.py:149
  215.2 1.5 gather_fusion.3
  216.7 1.3 fusion.44
  218.0 2.2 gather_fusion.4
  220.2 32.8 %all_to_all.37 = bf16[64,128,128]{2,1,0:T(8,128)(2,1)} all-to-all(bf16[64,128,128]{2,1,0:T(8,128)(2,1)} %gather_fusion.4), channel_id=1, replica_groups=mesh['exp'=16,'sky'=32] {'sky'}, dimensions={0} | all-to-all | bytes 4194304 | tf_op jit(solution)/shard_map/all_to_all | solution.py:111
  253.0 2.5 gather_fusion.5
  255.5 6.4 %fusion.3 = bf16[32,2,128,128]{3,2,1,0:T(8,128)(2,1)} fusion(bf16[1,32,2,128,128]{4,3,2,1,0:T(8,128)(2,1)} %param.8, f32[32,2]{1,0:T(8,128)S(1)} %copy.104, bf16[32,2,2,128,128]{4,3,2,1,0:T(8,128)(2,1)} %bitcast.192, bf16[32,128,128]{2,1,0:T(8,128)(2,1)S(1)} %gather_fusion.5), kind=kOutput, calls=%fused_computation.14 | convolution fusion | flops 542113792 | bytes 9437440 | tf_op jit(solution)/shard_map/fetv,fewv->fetw/dot_general | solution.py:47
  261.9 4.3 %bitcast_convert_fusion = bf16[32,128,128]{2,1,0:T(8,128)(2,1)S(1)} fusion(bf16[32,2,128,128]{3,2,1,0:T(8,128)(2,1)} %fusion.3, bf16[32,2,2,128,128]{4,3,2,1,0:T(8,128)(2,1)} %bitcast.193), kind=kOutput, calls=%fused_computation.20 | convolution fusion | flops 538443776 | bytes 7340032 | tf_op jit(solution)/shard_map/fetw,fewv->fetv/dot_general | solution.py:58
  266.2 2.3 gather_fusion.6
  268.4 1.8 broadcast_select_fusion
  270.2 31.9 %all_to_all.38 = bf16[64,128,128]{2,1,0:T(8,128)(2,1)S(1)} all-to-all(bf16[64,128,128]{2,1,0:T(8,128)(2,1)S(1)} %broadcast_select_fusion), channel_id=1, replica_groups=mesh['exp'=16,'sky'=32] {'sky'}, dimensions={0} | all-to-all | bytes 4194304 | tf_op jit(solution)/shard_map/all_to_all | solution.py:121
  302.2 1.3 fusion.30
  303.6 37.7 %all_to_all.39 = bf16[16,128,128]{2,1,0:T(8,128)(2,1)S(1)} all-to-all(bf16[16,128,128]{2,1,0:T(8,128)(2,1)S(1)} %copy.131), channel_id=1, replica_groups=mesh['exp'=16,'sky'=32] {'exp'}, dimensions={0} | all-to-all | bytes 1048576 | tf_op jit(solution)/shard_map/all_to_all | solution.py:134
  342.0 3.7 collective-permute-start.17
  345.7 4.9 %collective-permute-done.17 = bf16[1,128,128]{2,1,0:T(8,128)(2,1)S(1)} collective-permute-done((bf16[1,128,128]{2,1,0:T(8,128)(2,1)S(1)}, bf16[1,128,128]{2,1,0:T(8,128)(2,1)S(1)}, u32[]{:S(2)}, u32[]{:S(2)}) %collective-permute-start.17) | collective-permute-done | bytes 32800 | tf_op jit(solution)/shard_map/ppermute | solution.py:147
  350.5 1.9 collective-permute-start.18
  352.5 5.1 %collective-permute-start.25 = (bf16[1,128,128]{2,1,0:T(8,128)(2,1)S(1)}, bf16[1,128,128]{2,1,0:T(8,128)(2,1)S(1)}, u32[]{:S(2)}, u32[]{:S(2)}) collective-permute-start(bf16[1,128,128]{2,1,0:T(8,128)(2,1)S(1)} %fusion.61), channel_id=1, source_target_pairs={{32,0},{64,32},{96,64},{128,96},{160,128},{192,160},{224,192},{256... | collective-permute-start | bytes 98312 | tf_op jit(solution)/shard_map/ppermute | solution.py:149
  357.6 1.9 collective-permute-start.19
  359.5 5.1 %collective-permute-start.26 = (bf16[1,128,128]{2,1,0:T(8,128)(2,1)S(1)}, bf16[1,128,128]{2,1,0:T(8,128)(2,1)S(1)}, u32[]{:S(2)}, u32[]{:S(2)}) collective-permute-start(bf16[1,128,128]{2,1,0:T(8,128)(2,1)S(1)} %collective-permute-done.25), channel_id=1, source_target_pairs={{32,0},{64,32},{96,64},{128,96},{160,128},{192,160},{224,192},{256... | collective-permute-start | bytes 98312 | tf_op jit(solution)/shard_map/ppermute | solution.py:149
  364.7 1.9 collective-permute-start.20
  366.6 5.4 %collective-permute-start.27 = (bf16[1,128,128]{2,1,0:T(8,128)(2,1)S(1)}, bf16[1,128,128]{2,1,0:T(8,128)(2,1)S(1)}, u32[]{:S(2)}, u32[]{:S(2)}) collective-permute-start(bf16[1,128,128]{2,1,0:T(8,128)(2,1)S(1)} %collective-permute-done.26), channel_id=1, source_target_pairs={{32,0},{64,32},{96,64},{128,96},{160,128},{192,160},{224,192},{256... | collective-permute-start | bytes 98312 | tf_op jit(solution)/shard_map/ppermute | solution.py:149
  372.0 1.9 collective-permute-start.21
  374.0 5.1 %collective-permute-start.28 = (bf16[1,128,128]{2,1,0:T(8,128)(2,1)S(1)}, bf16[1,128,128]{2,1,0:T(8,128)(2,1)S(1)}, u32[]{:S(2)}, u32[]{:S(2)}) collective-permute-start(bf16[1,128,128]{2,1,0:T(8,128)(2,1)S(1)} %collective-permute-done.27), channel_id=1, source_target_pairs={{32,0},{64,32},{96,64},{128,96},{160,128},{192,160},{224,192},{256... | collective-permute-start | bytes 98312 | tf_op jit(solution)/shard_map/ppermute | solution.py:149
  379.1 1.9 collective-permute-start.22
  381.7 1.9 collective-permute-start.33
  384.0 2.4 collective-permute-start.32
  386.8 4.3 %collective-permute-done.32 = f32[16,128,1]{1,0,2:T(8,128)S(1)} collective-permute-done((f32[16,128,1]{1,0,2:T(8,128)S(1)}, f32[16,128,1]{1,0,2:T(8,128)S(1)}, u32[]{:S(2)}, u32[]{:S(2)}) %collective-permute-start.32) | collective-permute-done | bytes 8224 | tf_op jit(solution)/shard_map/ppermute | solution.py:24
  391.5 5.1 %collective-permute-start.29 = (bf16[1,128,128]{2,1,0:T(8,128)(2,1)S(1)}, bf16[1,128,128]{2,1,0:T(8,128)(2,1)S(1)}, u32[]{:S(2)}, u32[]{:S(2)}) collective-permute-start(bf16[1,128,128]{2,1,0:T(8,128)(2,1)S(1)} %collective-permute-done.28), channel_id=1, source_target_pairs={{32,0},{64,32},{96,64},{128,96},{160,128},{192,160},{224,192},{256... | collective-permute-start | bytes 98312 | tf_op jit(solution)/shard_map/ppermute | solution.py:149
  396.6 1.9 collective-permute-start.23
  399.8 5.1 %collective-permute-start.30 = (bf16[1,128,128]{2,1,0:T(8,128)(2,1)S(1)}, bf16[1,128,128]{2,1,0:T(8,128)(2,1)S(1)}, u32[]{:S(2)}, u32[]{:S(2)}) collective-permute-start(bf16[1,128,128]{2,1,0:T(8,128)(2,1)S(1)} %collective-permute-done.29), channel_id=1, source_target_pairs={{32,0},{64,32},{96,64},{128,96},{160,128},{192,160},{224,192},{256... | collective-permute-start | bytes 98312 | tf_op jit(solution)/shard_map/ppermute | solution.py:149
  404.9 1.9 collective-permute-start.24
  407.4 5.1 %collective-permute-start.31 = (bf16[1,128,128]{2,1,0:T(8,128)(2,1)S(1)}, bf16[1,128,128]{2,1,0:T(8,128)(2,1)S(1)}, u32[]{:S(2)}, u32[]{:S(2)}) collective-permute-start(bf16[1,128,128]{2,1,0:T(8,128)(2,1)S(1)} %collective-permute-done.30), channel_id=1, source_target_pairs={{32,0},{64,32},{96,64},{128,96},{160,128},{192,160},{224,192},{256... | collective-permute-start | bytes 98312 | tf_op jit(solution)/shard_map/ppermute | solution.py:149
  (149 shorter events, 24.2 us)
Async XLA Ops:
  19.3 3.3 copy-start.2
  22.6 5.3 %copy-start.13 = (bf16[1,32,2]{1,2,0:T(2,128)(2,1)S(1)}, bf16[1,32,2]{1,2,0:T(2,128)(2,1)}, u32[]{:S(2)}) copy-start(bf16[1,32,2]{1,2,0:T(2,128)(2,1)} %param.9) | copy-start | bytes 388
  22.6 5.4 %copy-start.10 = (s32[1,32,2,2]{1,3,2,0:T(2,128)S(1)}, s32[1,32,2,2]{1,3,2,0:T(2,128)}, u32[]{:S(2)}) copy-start(s32[1,32,2,2]{1,3,2,0:T(2,128)} %param.12) | copy-start | bytes 1540
  22.6 5.6 %copy-start.1 = (bf16[8,128,128]{2,1,0:T(8,128)(2,1)S(1)}, bf16[8,128,128]{2,1,0:T(8,128)(2,1)}, u32[]{:S(2)}) copy-start(bf16[8,128,128]{2,1,0:T(8,128)(2,1)} %param.13) | copy-start | bytes 786436
  22.6 31.8 %all-to-all-start.1 = ((bf16[64,128,128]{2,1,0:T(8,128)(2,1)}), bf16[64,128,128]{2,1,0:T(8,128)(2,1)S(1)}, u32[]{:S(2)}, u32[]{:S(2)}) async-start(bf16[64,128,128]{2,1,0:T(8,128)(2,1)} %gather_fusion), calls=%async_computation.1 | async-start | bytes 4194304 | tf_op jit(solution)/shard_map/all_to_all | solution.py:111
  29.6 3.2 copy-start.5
  32.8 27.4 %copy-start.4 = (s32[1024]{0:T(1024)}, s32[1024]{0:T(1024)S(1)}, u32[]{:S(2)}) copy-start(s32[1024]{0:T(1024)S(1)} %pad_clamp_fusion.2) | copy-start | bytes 12292
  32.8 31.0 %copy-start.3 = (s32[1024]{0:T(1024)}, s32[1024]{0:T(1024)S(1)}, u32[]{:S(2)}) copy-start(s32[1024]{0:T(1024)S(1)} %pad_clamp_fusion.1) | copy-start | bytes 12292
  32.8 32.0 %copy-start.8 = (pred[64]{0:T(512)(128)(4,1)}, pred[64]{0:T(512)(128)(4,1)S(1)}, u32[]{:S(2)}) copy-start(pred[64]{0:T(512)(128)(4,1)S(1)} %fusion.55) | copy-start | bytes 196
  66.4 45.0 %all-to-all-start.2 = ((bf16[64,128,128]{2,1,0:T(8,128)(2,1)}), bf16[64,128,128]{2,1,0:T(8,128)(2,1)S(1)}, u32[]{:S(2)}, u32[]{:S(2)}) async-start(bf16[64,128,128]{2,1,0:T(8,128)(2,1)} %broadcast_select_fusion.1), calls=%async_computation.2 | async-start | bytes 4194304 | tf_op jit(solution)/shard_map/all_to_all | solution.py:121
  75.9 37.8 %copy-start.6 = (s32[64]{0:T(128)}, s32[64]{0:T(128)S(1)}, u32[]{:S(2)}) copy-start(s32[64]{0:T(128)S(1)} %eq.67) | copy-start | bytes 772
  112.8 57.3 %copy-start = (f32[16,128,128]{2,1,0:T(8,128)S(1)}, f32[16,128,128]{2,1,0:T(8,128)}, u32[]{:S(2)}) copy-start(f32[16,128,128]{2,1,0:T(8,128)} %param.7) | copy-start | bytes 3145732
  113.7 32.5 %all-to-all-start.3 = ((bf16[16,128,128]{2,1,0:T(8,128)(2,1)}), bf16[16,128,128]{2,1,0:T(8,128)(2,1)S(1)}, u32[]{:S(2)}, u32[]{:S(2)}) async-start(bf16[16,128,128]{2,1,0:T(8,128)(2,1)} %copy.108), calls=%async_computation.3 | async-start | bytes 1048576 | tf_op jit(solution)/shard_map/all_to_all | solution.py:134
  120.6 47.5 %copy-start.11 = (f32[16]{0:T(128)}, f32[16]{0:T(128)S(1)}, u32[]{:S(2)}) copy-start(f32[16]{0:T(128)S(1)} %multiply_add_fusion) | copy-start | bytes 196
  146.9 7.0 %collective-permute-start = (bf16[1,128,128]{2,1,0:T(8,128)(2,1)S(1)}, bf16[1,128,128]{2,1,0:T(8,128)(2,1)S(1)}, u32[]{:S(2)}, u32[]{:S(2)}) collective-permute-start(bf16[1,128,128]{2,1,0:T(8,128)(2,1)S(1)} %fusion.60), channel_id=1, source_target_pairs={{0,32},{32,64},{64,96},{96,128},{128,160},{160,192},{192,224},{224... | collective-permute-start | bytes 98312 | tf_op jit(solution)/shard_map/ppermute | solution.py:147
  153.9 7.1 %collective-permute-start.1 = (bf16[1,128,128]{2,1,0:T(8,128)(2,1)S(1)}, bf16[1,128,128]{2,1,0:T(8,128)(2,1)S(1)}, u32[]{:S(2)}, u32[]{:S(2)}) collective-permute-start(bf16[1,128,128]{2,1,0:T(8,128)(2,1)S(1)} %collective-permute-done), channel_id=1, source_target_pairs={{0,32},{32,64},{64,96},{96,128},{128,160},{160,192},{192,224},{224... | collective-permute-start | bytes 98312 | tf_op jit(solution)/shard_map/ppermute | solution.py:147
  156.3 6.6 %collective-permute-start.8 = (bf16[1,128,128]{2,1,0:T(8,128)(2,1)S(1)}, bf16[1,128,128]{2,1,0:T(8,128)(2,1)S(1)}, u32[]{:S(2)}, u32[]{:S(2)}) collective-permute-start(bf16[1,128,128]{2,1,0:T(8,128)(2,1)S(1)} %fusion.60), channel_id=1, source_target_pairs={{32,0},{64,32},{96,64},{128,96},{160,128},{192,160},{224,192},{256... | collective-permute-start | bytes 98312 | tf_op jit(solution)/shard_map/ppermute | solution.py:149
  161.0 7.1 %collective-permute-start.2 = (bf16[1,128,128]{2,1,0:T(8,128)(2,1)S(1)}, bf16[1,128,128]{2,1,0:T(8,128)(2,1)S(1)}, u32[]{:S(2)}, u32[]{:S(2)}) collective-permute-start(bf16[1,128,128]{2,1,0:T(8,128)(2,1)S(1)} %collective-permute-done.1), channel_id=1, source_target_pairs={{0,32},{32,64},{64,96},{96,128},{128,160},{160,192},{192,224},{224... | collective-permute-start | bytes 98312 | tf_op jit(solution)/shard_map/ppermute | solution.py:147
  162.9 13.1 %collective-permute-start.9 = (bf16[1,128,128]{2,1,0:T(8,128)(2,1)S(1)}, bf16[1,128,128]{2,1,0:T(8,128)(2,1)S(1)}, u32[]{:S(2)}, u32[]{:S(2)}) collective-permute-start(bf16[1,128,128]{2,1,0:T(8,128)(2,1)S(1)} %collective-permute-done.8), channel_id=1, source_target_pairs={{32,0},{64,32},{96,64},{128,96},{160,128},{192,160},{224,192},{256... | collective-permute-start | bytes 98312 | tf_op jit(solution)/shard_map/ppermute | solution.py:149
  168.1 13.0 %collective-permute-start.3 = (bf16[1,128,128]{2,1,0:T(8,128)(2,1)S(1)}, bf16[1,128,128]{2,1,0:T(8,128)(2,1)S(1)}, u32[]{:S(2)}, u32[]{:S(2)}) collective-permute-start(bf16[1,128,128]{2,1,0:T(8,128)(2,1)S(1)} %collective-permute-done.2), channel_id=1, source_target_pairs={{0,32},{32,64},{64,96},{96,128},{128,160},{160,192},{192,224},{224... | collective-permute-start | bytes 98312 | tf_op jit(solution)/shard_map/ppermute | solution.py:147
  171.3 19.6 %collective-permute-start.16 = (f32[16,128,1]{1,0,2:T(8,128)}, f32[16,128,1]{1,0,2:T(8,128)S(1)}, u32[]{:S(2)}, u32[]{:S(2)}) collective-permute-start(f32[16,128,1]{1,0,2:T(8,128)} %copy.146), channel_id=1, source_target_pairs={{1,0},{2,1},{3,2},{4,3},{5,4},{6,5},{7,6},{8,7},{9,8},{10,9},{11,1... | collective-permute-start | bytes 24584 | tf_op jit(solution)/shard_map/ppermute | solution.py:26
  173.6 17.7 %collective-permute-start.15 = (f32[16,128,1]{1,0,2:T(8,128)S(1)}, f32[16,128,1]{1,0,2:T(8,128)}, u32[]{:S(2)}, u32[]{:S(2)}) collective-permute-start(f32[16,128,1]{1,0,2:T(8,128)S(1)} %copy.145), channel_id=1, source_target_pairs={{0,1},{1,2},{2,3},{3,4},{4,5},{5,6},{6,7},{7,8},{8,9},{9,10},{10,1... | collective-permute-start | bytes 24584 | tf_op jit(solution)/shard_map/ppermute | solution.py:24
  176.0 7.1 %collective-permute-start.10 = (bf16[1,128,128]{2,1,0:T(8,128)(2,1)S(1)}, bf16[1,128,128]{2,1,0:T(8,128)(2,1)S(1)}, u32[]{:S(2)}, u32[]{:S(2)}) collective-permute-start(bf16[1,128,128]{2,1,0:T(8,128)(2,1)S(1)} %collective-permute-done.9), channel_id=1, source_target_pairs={{32,0},{64,32},{96,64},{128,96},{160,128},{192,160},{224,192},{256... | collective-permute-start | bytes 98312 | tf_op jit(solution)/shard_map/ppermute | solution.py:149
  181.2 7.2 %collective-permute-start.4 = (bf16[1,128,128]{2,1,0:T(8,128)(2,1)S(1)}, bf16[1,128,128]{2,1,0:T(8,128)(2,1)S(1)}, u32[]{:S(2)}, u32[]{:S(2)}) collective-permute-start(bf16[1,128,128]{2,1,0:T(8,128)(2,1)S(1)} %collective-permute-done.3), channel_id=1, source_target_pairs={{0,32},{32,64},{64,96},{96,128},{128,160},{160,192},{192,224},{224... | collective-permute-start | bytes 98312 | tf_op jit(solution)/shard_map/ppermute | solution.py:147
  183.1 9.2 %collective-permute-start.11 = (bf16[1,128,128]{2,1,0:T(8,128)(2,1)S(1)}, bf16[1,128,128]{2,1,0:T(8,128)(2,1)S(1)}, u32[]{:S(2)}, u32[]{:S(2)}) collective-permute-start(bf16[1,128,128]{2,1,0:T(8,128)(2,1)S(1)} %collective-permute-done.10), channel_id=1, source_target_pairs={{32,0},{64,32},{96,64},{128,96},{160,128},{192,160},{224,192},{256... | collective-permute-start | bytes 98312 | tf_op jit(solution)/shard_map/ppermute | solution.py:149
  188.4 9.1 %collective-permute-start.5 = (bf16[1,128,128]{2,1,0:T(8,128)(2,1)S(1)}, bf16[1,128,128]{2,1,0:T(8,128)(2,1)S(1)}, u32[]{:S(2)}, u32[]{:S(2)}) collective-permute-start(bf16[1,128,128]{2,1,0:T(8,128)(2,1)S(1)} %collective-permute-done.4), channel_id=1, source_target_pairs={{0,32},{32,64},{64,96},{96,128},{128,160},{160,192},{192,224},{224... | collective-permute-start | bytes 98312 | tf_op jit(solution)/shard_map/ppermute | solution.py:147
  192.4 8.5 %collective-permute-start.12 = (bf16[1,128,128]{2,1,0:T(8,128)(2,1)S(1)}, bf16[1,128,128]{2,1,0:T(8,128)(2,1)S(1)}, u32[]{:S(2)}, u32[]{:S(2)}) collective-permute-start(bf16[1,128,128]{2,1,0:T(8,128)(2,1)S(1)} %collective-permute-done.11), channel_id=1, source_target_pairs={{32,0},{64,32},{96,64},{128,96},{160,128},{192,160},{224,192},{256... | collective-permute-start | bytes 98312 | tf_op jit(solution)/shard_map/ppermute | solution.py:149
  197.5 8.5 %collective-permute-start.6 = (bf16[1,128,128]{2,1,0:T(8,128)(2,1)S(1)}, bf16[1,128,128]{2,1,0:T(8,128)(2,1)S(1)}, u32[]{:S(2)}, u32[]{:S(2)}) collective-permute-start(bf16[1,128,128]{2,1,0:T(8,128)(2,1)S(1)} %collective-permute-done.5), channel_id=1, source_target_pairs={{0,32},{32,64},{64,96},{96,128},{128,160},{160,192},{192,224},{224... | collective-permute-start | bytes 98312 | tf_op jit(solution)/shard_map/ppermute | solution.py:147
  200.8 7.6 %collective-permute-start.13 = (bf16[1,128,128]{2,1,0:T(8,128)(2,1)S(1)}, bf16[1,128,128]{2,1,0:T(8,128)(2,1)S(1)}, u32[]{:S(2)}, u32[]{:S(2)}) collective-permute-start(bf16[1,128,128]{2,1,0:T(8,128)(2,1)S(1)} %collective-permute-done.12), channel_id=1, source_target_pairs={{32,0},{64,32},{96,64},{128,96},{160,128},{192,160},{224,192},{256... | collective-permute-start | bytes 98312 | tf_op jit(solution)/shard_map/ppermute | solution.py:149
  206.0 7.6 %collective-permute-start.7 = (bf16[1,128,128]{2,1,0:T(8,128)(2,1)S(1)}, bf16[1,128,128]{2,1,0:T(8,128)(2,1)S(1)}, u32[]{:S(2)}, u32[]{:S(2)}) collective-permute-start(bf16[1,128,128]{2,1,0:T(8,128)(2,1)S(1)} %collective-permute-done.6), channel_id=1, source_target_pairs={{0,32},{32,64},{64,96},{96,128},{128,160},{160,192},{192,224},{224... | collective-permute-start | bytes 98312 | tf_op jit(solution)/shard_map/ppermute | solution.py:147
  208.4 6.7 %collective-permute-start.14 = (bf16[1,128,128]{2,1,0:T(8,128)(2,1)S(1)}, bf16[1,128,128]{2,1,0:T(8,128)(2,1)S(1)}, u32[]{:S(2)}, u32[]{:S(2)}) collective-permute-start(bf16[1,128,128]{2,1,0:T(8,128)(2,1)S(1)} %collective-permute-done.13), channel_id=1, source_target_pairs={{32,0},{64,32},{96,64},{128,96},{160,128},{192,160},{224,192},{256... | collective-permute-start | bytes 98312 | tf_op jit(solution)/shard_map/ppermute | solution.py:149
  266.1 2.3 copy-start.9
  270.2 31.9 %copy-start.7 = (s32[64]{0:T(128)S(1)}, s32[64]{0:T(128)}, u32[]{:S(2)}) copy-start(s32[64]{0:T(128)} %copy-done.6) | copy-start | bytes 772
  342.0 8.5 %collective-permute-start.17 = (bf16[1,128,128]{2,1,0:T(8,128)(2,1)S(1)}, bf16[1,128,128]{2,1,0:T(8,128)(2,1)S(1)}, u32[]{:S(2)}, u32[]{:S(2)}) collective-permute-start(bf16[1,128,128]{2,1,0:T(8,128)(2,1)S(1)} %fusion.61), channel_id=1, source_target_pairs={{0,32},{32,64},{64,96},{96,128},{128,160},{160,192},{192,224},{224... | collective-permute-start | bytes 98312 | tf_op jit(solution)/shard_map/ppermute | solution.py:147
  350.5 7.1 %collective-permute-start.18 = (bf16[1,128,128]{2,1,0:T(8,128)(2,1)S(1)}, bf16[1,128,128]{2,1,0:T(8,128)(2,1)S(1)}, u32[]{:S(2)}, u32[]{:S(2)}) collective-permute-start(bf16[1,128,128]{2,1,0:T(8,128)(2,1)S(1)} %collective-permute-done.17), channel_id=1, source_target_pairs={{0,32},{32,64},{64,96},{96,128},{128,160},{160,192},{192,224},{224... | collective-permute-start | bytes 98312 | tf_op jit(solution)/shard_map/ppermute | solution.py:147
  352.5 7.1 %collective-permute-start.25 = (bf16[1,128,128]{2,1,0:T(8,128)(2,1)S(1)}, bf16[1,128,128]{2,1,0:T(8,128)(2,1)S(1)}, u32[]{:S(2)}, u32[]{:S(2)}) collective-permute-start(bf16[1,128,128]{2,1,0:T(8,128)(2,1)S(1)} %fusion.61), channel_id=1, source_target_pairs={{32,0},{64,32},{96,64},{128,96},{160,128},{192,160},{224,192},{256... | collective-permute-start | bytes 98312 | tf_op jit(solution)/shard_map/ppermute | solution.py:149
  357.6 7.1 %collective-permute-start.19 = (bf16[1,128,128]{2,1,0:T(8,128)(2,1)S(1)}, bf16[1,128,128]{2,1,0:T(8,128)(2,1)S(1)}, u32[]{:S(2)}, u32[]{:S(2)}) collective-permute-start(bf16[1,128,128]{2,1,0:T(8,128)(2,1)S(1)} %collective-permute-done.18), channel_id=1, source_target_pairs={{0,32},{32,64},{64,96},{96,128},{128,160},{160,192},{192,224},{224... | collective-permute-start | bytes 98312 | tf_op jit(solution)/shard_map/ppermute | solution.py:147
  359.5 7.1 %collective-permute-start.26 = (bf16[1,128,128]{2,1,0:T(8,128)(2,1)S(1)}, bf16[1,128,128]{2,1,0:T(8,128)(2,1)S(1)}, u32[]{:S(2)}, u32[]{:S(2)}) collective-permute-start(bf16[1,128,128]{2,1,0:T(8,128)(2,1)S(1)} %collective-permute-done.25), channel_id=1, source_target_pairs={{32,0},{64,32},{96,64},{128,96},{160,128},{192,160},{224,192},{256... | collective-permute-start | bytes 98312 | tf_op jit(solution)/shard_map/ppermute | solution.py:149
  364.7 7.3 %collective-permute-start.20 = (bf16[1,128,128]{2,1,0:T(8,128)(2,1)S(1)}, bf16[1,128,128]{2,1,0:T(8,128)(2,1)S(1)}, u32[]{:S(2)}, u32[]{:S(2)}) collective-permute-start(bf16[1,128,128]{2,1,0:T(8,128)(2,1)S(1)} %collective-permute-done.19), channel_id=1, source_target_pairs={{0,32},{32,64},{64,96},{96,128},{128,160},{160,192},{192,224},{224... | collective-permute-start | bytes 98312 | tf_op jit(solution)/shard_map/ppermute | solution.py:147
  366.6 7.3 %collective-permute-start.27 = (bf16[1,128,128]{2,1,0:T(8,128)(2,1)S(1)}, bf16[1,128,128]{2,1,0:T(8,128)(2,1)S(1)}, u32[]{:S(2)}, u32[]{:S(2)}) collective-permute-start(bf16[1,128,128]{2,1,0:T(8,128)(2,1)S(1)} %collective-permute-done.26), channel_id=1, source_target_pairs={{32,0},{64,32},{96,64},{128,96},{160,128},{192,160},{224,192},{256... | collective-permute-start | bytes 98312 | tf_op jit(solution)/shard_map/ppermute | solution.py:149
  372.0 7.1 %collective-permute-start.21 = (bf16[1,128,128]{2,1,0:T(8,128)(2,1)S(1)}, bf16[1,128,128]{2,1,0:T(8,128)(2,1)S(1)}, u32[]{:S(2)}, u32[]{:S(2)}) collective-permute-start(bf16[1,128,128]{2,1,0:T(8,128)(2,1)S(1)} %collective-permute-done.20), channel_id=1, source_target_pairs={{0,32},{32,64},{64,96},{96,128},{128,160},{160,192},{192,224},{224... | collective-permute-start | bytes 98312 | tf_op jit(solution)/shard_map/ppermute | solution.py:147
  374.0 17.5 %collective-permute-start.28 = (bf16[1,128,128]{2,1,0:T(8,128)(2,1)S(1)}, bf16[1,128,128]{2,1,0:T(8,128)(2,1)S(1)}, u32[]{:S(2)}, u32[]{:S(2)}) collective-permute-start(bf16[1,128,128]{2,1,0:T(8,128)(2,1)S(1)} %collective-permute-done.27), channel_id=1, source_target_pairs={{32,0},{64,32},{96,64},{128,96},{160,128},{192,160},{224,192},{256... | collective-permute-start | bytes 98312 | tf_op jit(solution)/shard_map/ppermute | solution.py:149
  379.1 17.5 %collective-permute-start.22 = (bf16[1,128,128]{2,1,0:T(8,128)(2,1)S(1)}, bf16[1,128,128]{2,1,0:T(8,128)(2,1)S(1)}, u32[]{:S(2)}, u32[]{:S(2)}) collective-permute-start(bf16[1,128,128]{2,1,0:T(8,128)(2,1)S(1)} %collective-permute-done.21), channel_id=1, source_target_pairs={{0,32},{32,64},{64,96},{96,128},{128,160},{160,192},{192,224},{224... | collective-permute-start | bytes 98312 | tf_op jit(solution)/shard_map/ppermute | solution.py:147
  381.7 4.7 %collective-permute-start.33 = (f32[16,128,1]{1,0,2:T(8,128)S(1)}, f32[16,128,1]{1,0,2:T(8,128)S(1)}, u32[]{:S(2)}, u32[]{:S(2)}) collective-permute-start(f32[16,128,1]{1,0,2:T(8,128)S(1)} %copy.133), channel_id=1, source_target_pairs={{1,0},{2,1},{3,2},{4,3},{5,4},{6,5},{7,6},{8,7},{9,8},{10,9},{11,1... | collective-permute-start | bytes 24584 | tf_op jit(solution)/shard_map/ppermute | solution.py:26
  384.0 7.1 %collective-permute-start.32 = (f32[16,128,1]{1,0,2:T(8,128)S(1)}, f32[16,128,1]{1,0,2:T(8,128)S(1)}, u32[]{:S(2)}, u32[]{:S(2)}) collective-permute-start(f32[16,128,1]{1,0,2:T(8,128)S(1)} %copy.132), channel_id=1, source_target_pairs={{0,1},{1,2},{2,3},{3,4},{4,5},{5,6},{6,7},{7,8},{8,9},{9,10},{10,1... | collective-permute-start | bytes 24584 | tf_op jit(solution)/shard_map/ppermute | solution.py:24
  391.5 8.3 %collective-permute-start.29 = (bf16[1,128,128]{2,1,0:T(8,128)(2,1)S(1)}, bf16[1,128,128]{2,1,0:T(8,128)(2,1)S(1)}, u32[]{:S(2)}, u32[]{:S(2)}) collective-permute-start(bf16[1,128,128]{2,1,0:T(8,128)(2,1)S(1)} %collective-permute-done.28), channel_id=1, source_target_pairs={{32,0},{64,32},{96,64},{128,96},{160,128},{192,160},{224,192},{256... | collective-permute-start | bytes 98312 | tf_op jit(solution)/shard_map/ppermute | solution.py:149
  396.6 8.3 %collective-permute-start.23 = (bf16[1,128,128]{2,1,0:T(8,128)(2,1)S(1)}, bf16[1,128,128]{2,1,0:T(8,128)(2,1)S(1)}, u32[]{:S(2)}, u32[]{:S(2)}) collective-permute-start(bf16[1,128,128]{2,1,0:T(8,128)(2,1)S(1)} %collective-permute-done.22), channel_id=1, source_target_pairs={{0,32},{32,64},{64,96},{96,128},{128,160},{160,192},{192,224},{224... | collective-permute-start | bytes 98312 | tf_op jit(solution)/shard_map/ppermute | solution.py:147
  399.8 7.6 %collective-permute-start.30 = (bf16[1,128,128]{2,1,0:T(8,128)(2,1)S(1)}, bf16[1,128,128]{2,1,0:T(8,128)(2,1)S(1)}, u32[]{:S(2)}, u32[]{:S(2)}) collective-permute-start(bf16[1,128,128]{2,1,0:T(8,128)(2,1)S(1)} %collective-permute-done.29), channel_id=1, source_target_pairs={{32,0},{64,32},{96,64},{128,96},{160,128},{192,160},{224,192},{256... | collective-permute-start | bytes 98312 | tf_op jit(solution)/shard_map/ppermute | solution.py:149
  404.9 7.6 %collective-permute-start.24 = (bf16[1,128,128]{2,1,0:T(8,128)(2,1)S(1)}, bf16[1,128,128]{2,1,0:T(8,128)(2,1)S(1)}, u32[]{:S(2)}, u32[]{:S(2)}) collective-permute-start(bf16[1,128,128]{2,1,0:T(8,128)(2,1)S(1)} %collective-permute-done.23), channel_id=1, source_target_pairs={{0,32},{32,64},{64,96},{96,128},{128,160},{160,192},{192,224},{224... | collective-permute-start | bytes 98312 | tf_op jit(solution)/shard_map/ppermute | solution.py:147
  407.4 7.5 %copy-start.12 = (f32[16]{0:T(128)S(1)}, f32[16]{0:T(128)}, u32[]{:S(2)}) copy-start(f32[16]{0:T(128)} %copy-done.11) | copy-start | bytes 196
  407.4 6.7 %collective-permute-start.31 = (bf16[1,128,128]{2,1,0:T(8,128)(2,1)S(1)}, bf16[1,128,128]{2,1,0:T(8,128)(2,1)S(1)}, u32[]{:S(2)}, u32[]{:S(2)}) collective-permute-start(bf16[1,128,128]{2,1,0:T(8,128)(2,1)S(1)} %collective-permute-done.30), channel_id=1, source_target_pairs={{32,0},{64,32},{96,64},{128,96},{160,128},{192,160},{224,192},{256... | collective-permute-start | bytes 98312 | tf_op jit(solution)/shard_map/ppermute | solution.py:149
